TPU v7x, 32 devices: a whole 2x2x4 slice. The times are simulated.
32 devices in a mesh: ox: 8 (over z, x), oy: 4 (over y, core).
Axes of the slice: x: 2, y: 2, z: 4, core: 2. Of those that a mesh axis runs over, the one named last changes fastest.
Arguments:
- atm_flux: bfloat16 [4, 40, 1024], P(None, 'oy', 'ox'), may hold values from -6 to 6
- remap_weights: bfloat16 [128, 12, 128, 128], P('ox', 'oy'), may hold values from -0.3125 to 0.3125
- tile_slots: int32 [128, 12], P('ox', 'oy'), may hold values from 0 to 23, as said below
- need_blocks: int32 [64, 12], P('ox', 'oy'), may hold values from -1 to 9, as said below
- send_blocks: int32 [64, 12], P('ox', 'oy'), may hold values from -1 to 9, as said below
- ocean_state: float32 [4, 16, 128, 512], P(None, None, 'ox', 'oy'), may hold values from -6 to 6
- land_mask: int32 [128, 512], P('ox', 'oy'), may hold values 0 or 1
- diffusivity: float32 [16], replicated, may hold values from 0.02 to 0.2
Outputs:
- ocean_final: float32 [4, 16, 128, 512], P(None, None, 'ox', 'oy')
- atmos_surface: float32 [40, 1024], P('oy', 'ox')
Inputs may be any that keep to these rules, and one draw needn't show every extreme that they name: `tile_slots`: entry [x, j * 3 + k] is q * 3 + s: the s-th block that owner q sends the ocean device of row x and latitude group j, with s below the number of blocks that owner sends it. `need_blocks`: entry [i * 8 + q, j * 3 + s] is the local block of owner (q, j) that ocean device (i, j) takes in place s, or -1; the first 1 to 3 places hold distinct blocks and the rest -1; every ocean device takes 3 blocks from some owner, and some device takes 3 from every owner. `send_blocks`: entry [q * 8 + i, j * 3 + s] equals need_blocks[i * 8 + q, j * 3 + s].
All inputs are finite; a program needn't handle non-finite values. No bound on the sum of `land_mask` on one device may be relied on, other than what follows from the above.
Results may differ from a plain program's by a relative error of at most 0.0022.
Values may be sent and summed in bfloat16 or wider, within the bound.
No kernel may reach another device: no remote copies, remote signals or barrier semaphores. Data moves between devices by JAX's collectives and lax.ppermute only.
A program may use at most 64 MiB of HBM per device.

v0:
```python
import jax
import jax.numpy as jnp
from jax import lax
from jax.sharding import PartitionSpec as P

STEPS = 3
advect_coef = 0.25
pressure_coef = 0.1
thermal_coef = 0.2
haline_coef = 0.8
coriolis_coef = 0.5
vertical_coef = 0.1
forcing_coef = 0.5


def with_halo(block, sides, width):
    for axis, dim in sides:
        count = lax.axis_size(axis)
        forward = [(i, i + 1) for i in range(count - 1)]
        backward = [(target, source) for source, target in forward]
        low = lax.ppermute(
            lax.slice_in_dim(block, block.shape[dim] - width, None, axis=dim), axis, forward
        )
        high = lax.ppermute(lax.slice_in_dim(block, 0, width, axis=dim), axis, backward)
        block = jnp.concatenate([low, block, high], axis=dim)
    return block


def advance(padded, center, diffusivity, coriolis, forcing, wetness):
    east = padded[:, :, 2:, 1:-1]
    west = padded[:, :, :-2, 1:-1]
    north = padded[:, :, 1:-1, 2:]
    south = padded[:, :, 1:-1, :-2]
    zonal = center[0]
    meridional = center[1]
    advection = (
        -advect_coef * 0.5 * (zonal[None] * (east - west) + meridional[None] * (north - south))
    )
    laplace = diffusivity[None, :, None, None] * (east + west + north + south - 4.0 * center)
    upper = jnp.concatenate([center[:, :1], center[:, :-1]], axis=1)
    lower = jnp.concatenate([center[:, 1:], center[:, -1:]], axis=1)
    mixing = vertical_coef * (upper + lower - 2.0 * center)
    density = haline_coef * padded[3] - thermal_coef * padded[2]
    pressure = jnp.cumsum(density, axis=0) - 0.5 * density
    grad_east = pressure[:, 2:, 1:-1] - pressure[:, :-2, 1:-1]
    grad_north = pressure[:, 1:-1, 2:] - pressure[:, 1:-1, :-2]
    zonal_push = coriolis * meridional - pressure_coef * 0.5 * grad_east
    merid_push = -coriolis * zonal - pressure_coef * 0.5 * grad_north
    tracer_zero = jnp.zeros((2,) + zonal.shape, jnp.float32)
    momentum = jnp.concatenate([zonal_push[None], merid_push[None], tracer_zero], axis=0)
    total = advection + laplace + mixing + momentum
    total = total.at[:, 0].add(forcing_coef * forcing)
    return center + wetness * total


def row_targets(tile_slots, need_blocks, capacity, owners):
    owner_of = tile_slots // capacity
    place_of = tile_slots % capacity
    return need_blocks[owner_of, place_of] * owners + owner_of


def lat_factor(first_cell, count, lat_total):
    latitude = (first_cell + jnp.arange(count, dtype=jnp.int32)).astype(jnp.float32)
    return coriolis_coef * (2.0 * (latitude + 0.5) / lat_total - 1.0)


def per_device(
    atm_flux,
    remap_weights,
    tile_slots,
    need_blocks,
    send_blocks,
    ocean_state,
    land_mask,
    diffusivity,
):
    flux_fields = atm_flux.shape[0]
    blocks_here = atm_flux.shape[1]
    block_width = atm_flux.shape[2]
    owners = lax.axis_size("ox")
    tile_count = tile_slots.shape[0]
    refs_tile = tile_slots.shape[1]
    capacity = send_blocks.shape[1]
    whole = lax.all_gather(atm_flux, "ox", axis=2, tiled=True)
    table = whole.reshape(flux_fields, blocks_here * owners, block_width)
    picks = table[:, row_targets(tile_slots, need_blocks, capacity, owners)]
    forcing = jnp.einsum("ftka,tkra->ftr", picks, remap_weights, preferred_element_type=jnp.float32)
    lat_cells = ocean_state.shape[3]
    lat_total = lat_cells * lax.axis_size("oy")
    lat_start = lax.axis_index("oy") * lat_cells
    wetness = land_mask.astype(jnp.float32)
    state = ocean_state
    coriolis = lat_factor(lat_start, lat_cells, lat_total)
    for repeat in range(STEPS):
        padded = with_halo(state, (("ox", 2), ("oy", 3)), 1)
        state = advance(padded, state, diffusivity, coriolis, forcing, wetness)
    surface = state[2, 0].astype(jnp.bfloat16)
    pieces = jnp.einsum("tkra,tr->tka", remap_weights, surface, preferred_element_type=jnp.float32)
    pieces = pieces.reshape(tile_count * refs_tile, block_width)
    targets = row_targets(tile_slots, need_blocks, capacity, owners).reshape(-1)
    segment_line = jnp.arange(blocks_here * owners, dtype=jnp.int32)
    select = (targets[:, None] == segment_line[None, :]).astype(jnp.float32)
    dense = lax.dot_general(
        select, pieces, (((0,), (0,)), ((), ())), precision=lax.Precision.HIGHEST
    )
    dense = dense.reshape(blocks_here, owners * block_width)
    atmos_surface = lax.psum_scatter(dense, "ox", scatter_dimension=1, tiled=True)
    return (state, atmos_surface)


def solution(mesh):
    return jax.shard_map(
        per_device,
        mesh=mesh,
        in_specs=(
            P(None, "oy", "ox"),
            P("ox", "oy", None, None),
            P("ox", "oy"),
            P("ox", "oy"),
            P("ox", "oy"),
            P(None, None, "ox", "oy"),
            P("ox", "oy"),
            P(),
        ),
        out_specs=(P(None, None, "ox", "oy"), P("oy", "ox")),
        check_vma=False,
    )
```

profile of v0, /device:TPU:0, one launch (start us, length us, event | category | flops | bytes accessed | tf_op | source)
XLA Modules:
  0.0 182.9 jit_solution(17034254981242002225)
XLA Ops:
  7.2 1.2 fusion.83
  8.4 4.8 %collective-permute-start.1 = (f32[4,16,1,128]{3,2,1,0:T(1,128)S(1)}, f32[4,16,1,128]{3,2,1,0:T(1,128)S(1)}, u32[]{:S(2)}, u32[]{:S(2)}) collective-permute-start(f32[4,16,1,128]{3,2,1,0:T(1,128)S(1)} %get-tuple-element.76), channel_id=1, source_target_pairs={{0,4},{4,8},{8,12},{12,16},{16,20},{20,24},{24,28},{1,5},{5,9},{9,... | collective-permute-start | bytes 98312 | tf_op jit(solution)/shard_map/ppermute | solution.py:21
  13.3 1.3 collective-permute-start
  15.4 1.7 slice_bitcast_fusion.5
  17.1 2.1 %fusion.84 = (f32[4,15,16,128]{3,2,1,0:T(8,128)S(1)}, f32[4,15,16,128]{3,2,1,0:T(8,128)}) fusion(f32[4,16,16,128]{3,2,1,0:T(8,128)} %param.18), kind=kLoop, calls=%fused_computation.163 | loop fusion | bytes 1966080 | tf_op jit(solution)/shard_map/slice | solution.py:41
  20.7 22.4 %all_gather.3 = bf16[4,10,1024]{2,0,1:T(4,128)(2,1)S(1)} all-gather(bf16[4,10,128]{2,0,1:T(4,128)(2,1)S(1)} %copy-done.16), channel_id=1, replica_groups=mesh['ox'=8,'oy'=4] {'ox'}, dimensions={2}, use_global_device_ids=true | all-gather | bytes 92160 | tf_op jit(solution)/shard_map/all_gather | solution.py:84
  44.5 1.2 fusion.76
  45.7 2.2 %copy.144 = f32[4,16,18,1]{2,1,3,0:T(8,128)} copy(f32[4,16,18,1]{3,2,1,0:T(8,128)} %get-tuple-element.56) | data formatting | bytes 9216 | tf_op jit(solution)/shard_map/slice | solution.py:22
  49.0 1.3 collective-permute-start.2
  50.2 3.6 %collective-permute-start.3 = (f32[4,16,18,1]{2,1,3,0:T(8,128)}, f32[4,16,18,1]{2,1,3,0:T(8,128)}, u32[]{:S(2)}, u32[]{:S(2)}) collective-permute-start(f32[4,16,18,1]{2,1,3,0:T(8,128)} %copy.144), channel_id=1, source_target_pairs={{0,1},{1,2},{2,3},{4,5},{5,6},{6,7},{8,9},{9,10},{10,11},{12,13},{... | collective-permute-start | bytes 13832 | tf_op jit(solution)/shard_map/ppermute | solution.py:21
  56.5 1.3 copy.145
  57.7 2.1 %copy.143 = f32[4,16,18,1]{3,2,1,0:T(8,128)} copy(f32[4,16,18,1]{2,1,3,0:T(8,128)} %collective-permute-done.2) | data formatting | bytes 9216 | tf_op jit(solution)/shard_map/ppermute | solution.py:24
  59.9 2.2 %reduce-window_subtract_fusion.2 = f32[16,18,130]{2,1,0:T(8,128)S(1)} fusion(f32[4,16,18,1]{3,2,1,0:T(8,128)} %copy.143, f32[4,16,1,128]{3,2,1,0:T(1,128)S(1)} %collective-permute-done, f32[4,16,16,128]{3,2,1,0:T(8,128)S(1)} %copy-done.2, f32[4,16,1,128]{3,2,1,0:T(1,128)S(1)} %collective-permute-done.1, f32[4,16,18,1]{3,2,1,0:T(8,128)S(1)} %copy.145), kind=kOutput, calls=%fused_computation.4 | output fusion | flops 1460160 | bytes 748800 | tf_op jit(solution)/shard_map/jit(cumsum)/reduce_window_sum | solution.py:44
  65.2 1.3 collective-permute-start.5
  66.5 1.3 collective-permute-start.4
  68.5 3.8 %collective-permute-done.4 = f32[4,16,1,128]{3,2,1,0:T(1,128)S(1)} collective-permute-done((f32[4,16,1,128]{3,2,1,0:T(1,128)S(1)}, f32[4,16,1,128]{3,2,1,0:T(1,128)S(1)}, u32[]{:S(2)}, u32[]{:S(2)}) %collective-permute-start.4) | collective-permute-done | bytes 32800 | tf_op jit(solution)/shard_map/ppermute | solution.py:24
  73.6 2.2 %copy.156 = f32[4,16,18,1]{2,1,3,0:T(8,128)} copy(f32[4,16,18,1]{3,2,1,0:T(8,128)} %get-tuple-element.54) | data formatting | bytes 9216 | tf_op jit(solution)/shard_map/slice | solution.py:22
  76.9 1.3 collective-permute-start.6
  78.2 3.6 %collective-permute-start.7 = (f32[4,16,18,1]{2,1,3,0:T(8,128)}, f32[4,16,18,1]{2,1,3,0:T(8,128)}, u32[]{:S(2)}, u32[]{:S(2)}) collective-permute-start(f32[4,16,18,1]{2,1,3,0:T(8,128)} %copy.156), channel_id=1, source_target_pairs={{0,1},{1,2},{2,3},{4,5},{5,6},{6,7},{8,9},{9,10},{10,11},{12,13},{... | collective-permute-start | bytes 13832 | tf_op jit(solution)/shard_map/ppermute | solution.py:21
  82.4 1.3 copy.157
  83.6 2.1 %copy.155 = f32[4,16,18,1]{3,2,1,0:T(8,128)} copy(f32[4,16,18,1]{2,1,3,0:T(8,128)} %collective-permute-done.6) | data formatting | bytes 9216 | tf_op jit(solution)/shard_map/ppermute | solution.py:24
  85.8 2.2 %reduce-window_subtract_fusion.1 = f32[16,18,130]{2,1,0:T(8,128)S(1)} fusion(f32[4,16,18,1]{3,2,1,0:T(8,128)} %copy.155, f32[4,16,1,128]{3,2,1,0:T(1,128)S(1)} %collective-permute-done.4, f32[4,16,16,128]{3,2,1,0:T(8,128)S(1)} %multiply_add_fusion.2, f32[4,16,1,128]{3,2,1,0:T(1,128)S(1)} %collective-permute-done.5, f32[4,16,18,1]{3,2,1,0:T(8,128)S(1)} %copy.157), kind=kOutput, calls=%fused_computation.3 | output fusion | flops 1460160 | bytes 748800 | tf_op jit(solution)/shard_map/jit(cumsum)/reduce_window_sum | solution.py:44
  91.1 3.6 %collective-permute-start.9 = (f32[4,16,1,128]{3,2,1,0:T(1,128)S(1)}, f32[4,16,1,128]{3,2,1,0:T(1,128)S(1)}, u32[]{:S(2)}, u32[]{:S(2)}) collective-permute-start(f32[4,16,1,128]{3,2,1,0:T(1,128)S(1)} %get-tuple-element.60), channel_id=1, source_target_pairs={{0,4},{4,8},{8,12},{12,16},{16,20},{20,24},{24,28},{1,5},{5,9},{9,... | collective-permute-start | bytes 98312 | tf_op jit(solution)/shard_map/ppermute | solution.py:21
  94.7 1.3 collective-permute-start.8
  96.7 4.1 %collective-permute-done.8 = f32[4,16,1,128]{3,2,1,0:T(1,128)S(1)} collective-permute-done((f32[4,16,1,128]{3,2,1,0:T(1,128)S(1)}, f32[4,16,1,128]{3,2,1,0:T(1,128)S(1)}, u32[]{:S(2)}, u32[]{:S(2)}) %collective-permute-start.8) | collective-permute-done | bytes 32800 | tf_op jit(solution)/shard_map/ppermute | solution.py:24
  102.2 2.2 %copy.162 = f32[4,16,18,1]{2,1,3,0:T(8,128)} copy(f32[4,16,18,1]{3,2,1,0:T(8,128)} %get-tuple-element.52) | data formatting | bytes 9216 | tf_op jit(solution)/shard_map/slice | solution.py:22
  105.5 1.3 collective-permute-start.10
  106.7 3.6 %collective-permute-start.11 = (f32[4,16,18,1]{2,1,3,0:T(8,128)}, f32[4,16,18,1]{2,1,3,0:T(8,128)}, u32[]{:S(2)}, u32[]{:S(2)}) collective-permute-start(f32[4,16,18,1]{2,1,3,0:T(8,128)} %copy.162), channel_id=1, source_target_pairs={{0,1},{1,2},{2,3},{4,5},{5,6},{6,7},{8,9},{9,10},{10,11},{12,13},{... | collective-permute-start | bytes 13832 | tf_op jit(solution)/shard_map/ppermute | solution.py:21
  111.0 1.3 copy.163
  112.2 2.1 %copy.161 = f32[4,16,18,1]{3,2,1,0:T(8,128)} copy(f32[4,16,18,1]{2,1,3,0:T(8,128)} %collective-permute-done.10) | data formatting | bytes 9216 | tf_op jit(solution)/shard_map/ppermute | solution.py:24
  114.4 2.2 %reduce-window_subtract_fusion = f32[16,18,130]{2,1,0:T(8,128)S(1)} fusion(f32[4,16,18,1]{3,2,1,0:T(8,128)} %copy.161, f32[4,16,1,128]{3,2,1,0:T(1,128)S(1)} %collective-permute-done.8, f32[4,16,16,128]{3,2,1,0:T(8,128)S(1)} %multiply_add_fusion.1, f32[4,16,1,128]{3,2,1,0:T(1,128)S(1)} %collective-permute-done.9, f32[4,16,18,1]{3,2,1,0:T(8,128)S(1)} %copy.163), kind=kOutput, calls=%fused_computation.2 | output fusion | flops 1460160 | bytes 748800 | tf_op jit(solution)/shard_map/jit(cumsum)/reduce_window_sum | solution.py:44
  120.3 55.7 %reduce-scatter.2.cloned.1.call-done = f32[10,128]{1,0:T(8,128)} async-done(((f32[10,1024]{1,0:T(8,128)}), f32[10,128]{1,0:T(8,128)}) %reduce-scatter.2.cloned.1.call-update) | async-done | bytes 5136 | tf_op jit(solution)/shard_map/reduce_scatter | solution.py:107
  (117 shorter events, 24.2 us)
Async XLA Ops:
  7.2 36.5 %copy-start = (bf16[16,3,128,128]{3,2,1,0:T(8,128)(2,1)S(1)}, bf16[16,3,128,128]{3,2,1,0:T(8,128)(2,1)}, u32[]{:S(2)}) copy-start(bf16[16,3,128,128]{3,2,1,0:T(8,128)(2,1)} %param.15) | copy-start | bytes 4718596
  7.2 12.0 %copy-start.26 = (s32[16,3]{0,1:T(4,128)S(1)}, s32[16,3]{0,1:T(4,128)}, u32[]{:S(2)}) copy-start(s32[16,3]{0,1:T(4,128)} %param.16) | copy-start | bytes 580
  7.2 12.2 %copy-start.1 = (s32[8,3]{0,1:T(4,128)S(1)}, s32[8,3]{0,1:T(4,128)}, u32[]{:S(2)}) copy-start(s32[8,3]{0,1:T(4,128)} %param.17) | copy-start | bytes 292
  7.2 168.8 %reduce-scatter.2.cloned.1.call-start = ((), (), s32[]{:S(2)}) async-start(), calls=%async_computation.1 | async-start | bytes 73728 | tf_op jit(solution)/shard_map/reduce_scatter | solution.py:107
  8.4 35.9 %collective-permute-start.1 = (f32[4,16,1,128]{3,2,1,0:T(1,128)S(1)}, f32[4,16,1,128]{3,2,1,0:T(1,128)S(1)}, u32[]{:S(2)}, u32[]{:S(2)}) collective-permute-start(f32[4,16,1,128]{3,2,1,0:T(1,128)S(1)} %get-tuple-element.76), channel_id=1, source_target_pairs={{0,4},{4,8},{8,12},{12,16},{16,20},{20,24},{24,28},{1,5},{5,9},{9,... | collective-permute-start | bytes 98312 | tf_op jit(solution)/shard_map/ppermute | solution.py:21
  13.3 31.0 %collective-permute-start = (f32[4,16,1,128]{3,2,1,0:T(1,128)S(1)}, f32[4,16,1,128]{3,2,1,0:T(1,128)S(1)}, u32[]{:S(2)}, u32[]{:S(2)}) collective-permute-start(f32[4,16,1,128]{3,2,1,0:T(1,128)S(1)} %get-tuple-element.77), channel_id=1, source_target_pairs={{4,0},{8,4},{12,8},{16,12},{20,16},{24,20},{28,24},{5,1},{9,5},{13... | collective-permute-start | bytes 98312 | tf_op jit(solution)/shard_map/ppermute | solution.py:24
  20.4 23.9 %copy-start.2 = (f32[4,16,16,128]{3,2,1,0:T(8,128)S(1)}, f32[4,16,16,128]{3,2,1,0:T(8,128)}, u32[]{:S(2)}) copy-start(f32[4,16,16,128]{3,2,1,0:T(8,128)} %param.18) | copy-start | bytes 1572868
  49.0 8.8 %collective-permute-start.2 = (f32[4,16,18,1]{2,1,3,0:T(8,128)}, f32[4,16,18,1]{2,1,3,0:T(8,128)}, u32[]{:S(2)}, u32[]{:S(2)}) collective-permute-start(f32[4,16,18,1]{2,1,3,0:T(8,128)} %copy.142), channel_id=1, source_target_pairs={{1,0},{2,1},{3,2},{5,4},{6,5},{7,6},{9,8},{10,9},{11,10},{13,12},{... | collective-permute-start | bytes 13832 | tf_op jit(solution)/shard_map/ppermute | solution.py:24
  50.2 6.2 %collective-permute-start.3 = (f32[4,16,18,1]{2,1,3,0:T(8,128)}, f32[4,16,18,1]{2,1,3,0:T(8,128)}, u32[]{:S(2)}, u32[]{:S(2)}) collective-permute-start(f32[4,16,18,1]{2,1,3,0:T(8,128)} %copy.144), channel_id=1, source_target_pairs={{0,1},{1,2},{2,3},{4,5},{5,6},{6,7},{8,9},{9,10},{10,11},{12,13},{... | collective-permute-start | bytes 13832 | tf_op jit(solution)/shard_map/ppermute | solution.py:21
  59.9 2.5 %copy-start.6 = (f32[4,15,16,128]{3,2,1,0:T(8,128)S(1)}, f32[4,15,16,128]{3,2,1,0:T(8,128)}, u32[]{:S(2)}) copy-start(f32[4,15,16,128]{3,2,1,0:T(8,128)} %get-tuple-element.79) | copy-start | bytes 1474564
  59.9 2.5 %copy-start.10 = (f32[16,16,128]{2,1,0:T(8,128)S(1)}, f32[16,16,128]{2,1,0:T(8,128)}, u32[]{:S(2)}) copy-start(f32[16,16,128]{2,1,0:T(8,128)} %get-tuple-element.74) | copy-start | bytes 393220
  59.9 2.5 %copy-start.11 = (f32[16,16,128]{2,1,0:T(8,128)S(1)}, f32[16,16,128]{2,1,0:T(8,128)}, u32[]{:S(2)}) copy-start(f32[16,16,128]{2,1,0:T(8,128)} %get-tuple-element.75) | copy-start | bytes 393220
  59.9 2.5 %copy-start.19 = (f32[16]{0:T(128)S(1)}, f32[16]{0:T(128)}, u32[]{:S(2)}) copy-start(f32[16]{0:T(128)} %param.20) | copy-start | bytes 196
  59.9 2.5 %copy-start.22 = (f32[4]{0:T(128)S(1)}, f32[4]{0:T(128)}, u32[]{:S(2)}) copy-start(f32[4]{0:T(128)} %pad.62.clone) | copy-start | bytes 52
  65.2 3.3 %collective-permute-start.5 = (f32[4,16,1,128]{3,2,1,0:T(1,128)S(1)}, f32[4,16,1,128]{3,2,1,0:T(1,128)S(1)}, u32[]{:S(2)}, u32[]{:S(2)}) collective-permute-start(f32[4,16,1,128]{3,2,1,0:T(1,128)S(1)} %get-tuple-element.68), channel_id=1, source_target_pairs={{0,4},{4,8},{8,12},{12,16},{16,20},{20,24},{24,28},{1,5},{5,9},{9,... | collective-permute-start | bytes 98312 | tf_op jit(solution)/shard_map/ppermute | solution.py:21
  66.5 5.8 %collective-permute-start.4 = (f32[4,16,1,128]{3,2,1,0:T(1,128)S(1)}, f32[4,16,1,128]{3,2,1,0:T(1,128)S(1)}, u32[]{:S(2)}, u32[]{:S(2)}) collective-permute-start(f32[4,16,1,128]{3,2,1,0:T(1,128)S(1)} %get-tuple-element.69), channel_id=1, source_target_pairs={{4,0},{8,4},{12,8},{16,12},{20,16},{24,20},{28,24},{5,1},{9,5},{13... | collective-permute-start | bytes 98312 | tf_op jit(solution)/shard_map/ppermute | solution.py:24
  76.9 6.8 %collective-permute-start.6 = (f32[4,16,18,1]{2,1,3,0:T(8,128)}, f32[4,16,18,1]{2,1,3,0:T(8,128)}, u32[]{:S(2)}, u32[]{:S(2)}) collective-permute-start(f32[4,16,18,1]{2,1,3,0:T(8,128)} %copy.154), channel_id=1, source_target_pairs={{1,0},{2,1},{3,2},{5,4},{6,5},{7,6},{9,8},{10,9},{11,10},{13,12},{... | collective-permute-start | bytes 13832 | tf_op jit(solution)/shard_map/ppermute | solution.py:24
  78.2 4.2 %collective-permute-start.7 = (f32[4,16,18,1]{2,1,3,0:T(8,128)}, f32[4,16,18,1]{2,1,3,0:T(8,128)}, u32[]{:S(2)}, u32[]{:S(2)}) collective-permute-start(f32[4,16,18,1]{2,1,3,0:T(8,128)} %copy.156), channel_id=1, source_target_pairs={{0,1},{1,2},{2,3},{4,5},{5,6},{6,7},{8,9},{9,10},{10,11},{12,13},{... | collective-permute-start | bytes 13832 | tf_op jit(solution)/shard_map/ppermute | solution.py:21
  85.8 2.4 %copy-start.8 = (f32[4,15,16,128]{3,2,1,0:T(8,128)S(1)}, f32[4,15,16,128]{3,2,1,0:T(8,128)}, u32[]{:S(2)}) copy-start(f32[4,15,16,128]{3,2,1,0:T(8,128)} %get-tuple-element.71) | copy-start | bytes 1474564
  85.8 2.4 %copy-start.14 = (f32[16,16,128]{2,1,0:T(8,128)S(1)}, f32[16,16,128]{2,1,0:T(8,128)}, u32[]{:S(2)}) copy-start(f32[16,16,128]{2,1,0:T(8,128)} %get-tuple-element.66) | copy-start | bytes 393220
  85.8 2.5 %copy-start.15 = (f32[16,16,128]{2,1,0:T(8,128)S(1)}, f32[16,16,128]{2,1,0:T(8,128)}, u32[]{:S(2)}) copy-start(f32[16,16,128]{2,1,0:T(8,128)} %get-tuple-element.67) | copy-start | bytes 393220
  85.8 2.5 %copy-start.20 = (f32[16]{0:T(128)S(1)}, f32[16]{0:T(128)}, u32[]{:S(2)}) copy-start(f32[16]{0:T(128)} %param.20) | copy-start | bytes 196
  85.8 2.5 %copy-start.23 = (f32[4]{0:T(128)S(1)}, f32[4]{0:T(128)}, u32[]{:S(2)}) copy-start(f32[4]{0:T(128)} %pad.62.clone) | copy-start | bytes 52
  91.1 5.7 %collective-permute-start.9 = (f32[4,16,1,128]{3,2,1,0:T(1,128)S(1)}, f32[4,16,1,128]{3,2,1,0:T(1,128)S(1)}, u32[]{:S(2)}, u32[]{:S(2)}) collective-permute-start(f32[4,16,1,128]{3,2,1,0:T(1,128)S(1)} %get-tuple-element.60), channel_id=1, source_target_pairs={{0,4},{4,8},{8,12},{12,16},{16,20},{20,24},{24,28},{1,5},{5,9},{9,... | collective-permute-start | bytes 98312 | tf_op jit(solution)/shard_map/ppermute | solution.py:21
  94.7 6.1 %collective-permute-start.8 = (f32[4,16,1,128]{3,2,1,0:T(1,128)S(1)}, f32[4,16,1,128]{3,2,1,0:T(1,128)S(1)}, u32[]{:S(2)}, u32[]{:S(2)}) collective-permute-start(f32[4,16,1,128]{3,2,1,0:T(1,128)S(1)} %get-tuple-element.61), channel_id=1, source_target_pairs={{4,0},{8,4},{12,8},{16,12},{20,16},{24,20},{28,24},{5,1},{9,5},{13... | collective-permute-start | bytes 98312 | tf_op jit(solution)/shard_map/ppermute | solution.py:24
  105.5 6.8 %collective-permute-start.10 = (f32[4,16,18,1]{2,1,3,0:T(8,128)}, f32[4,16,18,1]{2,1,3,0:T(8,128)}, u32[]{:S(2)}, u32[]{:S(2)}) collective-permute-start(f32[4,16,18,1]{2,1,3,0:T(8,128)} %copy.160), channel_id=1, source_target_pairs={{1,0},{2,1},{3,2},{5,4},{6,5},{7,6},{9,8},{10,9},{11,10},{13,12},{... | collective-permute-start | bytes 13832 | tf_op jit(solution)/shard_map/ppermute | solution.py:24
  106.7 4.2 %collective-permute-start.11 = (f32[4,16,18,1]{2,1,3,0:T(8,128)}, f32[4,16,18,1]{2,1,3,0:T(8,128)}, u32[]{:S(2)}, u32[]{:S(2)}) collective-permute-start(f32[4,16,18,1]{2,1,3,0:T(8,128)} %copy.162), channel_id=1, source_target_pairs={{0,1},{1,2},{2,3},{4,5},{5,6},{6,7},{8,9},{9,10},{10,11},{12,13},{... | collective-permute-start | bytes 13832 | tf_op jit(solution)/shard_map/ppermute | solution.py:21
  114.4 2.4 %copy-start.12 = (f32[16,16,128]{2,1,0:T(8,128)S(1)}, f32[16,16,128]{2,1,0:T(8,128)}, u32[]{:S(2)}) copy-start(f32[16,16,128]{2,1,0:T(8,128)} %get-tuple-element.58) | copy-start | bytes 393220
  114.4 2.5 %copy-start.13 = (f32[16,16,128]{2,1,0:T(8,128)S(1)}, f32[16,16,128]{2,1,0:T(8,128)}, u32[]{:S(2)}) copy-start(f32[16,16,128]{2,1,0:T(8,128)} %get-tuple-element.59) | copy-start | bytes 393220
  114.4 2.5 %copy-start.21 = (f32[16]{0:T(128)S(1)}, f32[16]{0:T(128)}, u32[]{:S(2)}) copy-start(f32[16]{0:T(128)} %param.20) | copy-start | bytes 196
  114.4 2.5 %copy-start.24 = (f32[4]{0:T(128)S(1)}, f32[4]{0:T(128)}, u32[]{:S(2)}) copy-start(f32[4]{0:T(128)} %pad.62.clone) | copy-start | bytes 52
  118.8 57.2 %copy-start.9 = (f32[4,16,16,128]{3,2,1,0:T(8,128)}, f32[4,16,16,128]{3,2,1,0:T(8,128)S(1)}, u32[]{:S(2)}) copy-start(f32[4,16,16,128]{3,2,1,0:T(8,128)S(1)} %multiply_add_fusion) | copy-start | bytes 1572868
  (8 other events, 12.4 us)
Sparse Core Ops, SparseCore 0:
  120.4 55.5 reduce-scatter.1
where the time goes:
time: 184 us; the launch traced here: 183 us
  waiting for transfers between devices  64.8 us (35%)
  local copies, waits for them, and re-layouts  39.6 us (22%)
  starting transfers between devices  28.5 us (15%)
  blocking collectives  22.4 us (12%)
  between operations  14.6 us (8%)
  other arithmetic  11.8 us (6%)
    reduce_scatter x1, waiting for transfers between devices, per_device(): lax.psum_scatter(dense, 'ox', scatter_dimension=1, tiled=True)  55.7 us
    all_gather x1, blocking collectives, per_device(): whole = lax.all_gather(atm_flux, 'ox', axis=2, tiled=True)  22.4 us
    ppermute x6, starting transfers between devices, with_halo(): lax.ppermute(lax.slice_in_dim(block, block.shape[dim] - width, None, axis...  20.7 us
    slice x9, local copies, waits for them, and re-layouts, with_halo(): lax.slice_in_dim(block, block.shape[dim] - width, None, axis=dim)  11.5 us
    ppermute x6, waiting for transfers between devices, with_halo(): lax.ppermute(lax.slice_in_dim(block, 0, width, axis=dim), axis, backward)  7.92 us
    ppermute x6, starting transfers between devices, with_halo(): lax.ppermute(lax.slice_in_dim(block, 0, width, axis=dim), axis, backward)  7.72 us
    another operation x3, other arithmetic, advance(): pressure = jnp.cumsum(density, axis=0) - 0.5 * density  6.68 us
    ppermute x3, local copies, waits for them, and re-layouts, with_halo(): lax.ppermute(lax.slice_in_dim(block, 0, width, axis=dim), axis, backward)  6.43 us
  transfers between devices with their start and end apart: 13, of which 5 were waited for; matrix products, arithmetic and copies ran while one was open for 8% of the time, Pallas kernels for 0%

commit v1 on v0

--- a/solution.py
+++ b/solution.py
@@ -81,7 +81,14 @@
     tile_count = tile_slots.shape[0]
     refs_tile = tile_slots.shape[1]
     capacity = send_blocks.shape[1]
-    whole = lax.all_gather(atm_flux, "ox", axis=2, tiled=True)
+    size = lax.axis_size("ox")
+    forward_2 = [(i_2, (i_2 + 1) % size) for i_2 in range(size)]
+    parts = [atm_flux]
+    for hop in range(1, size):
+        parts = [lax.ppermute(parts[0], "ox", forward_2), *parts]
+    full = jnp.concatenate(parts, axis=2)
+    shift = (lax.axis_index("ox") + 1) * parts[-1].shape[2]
+    whole = jnp.roll(full, shift, axis=2)
     table = whole.reshape(flux_fields, blocks_here * owners, block_width)
     picks = table[:, row_targets(tile_slots, need_blocks, capacity, owners)]
     forcing = jnp.einsum("ftka,tkra->ftr", picks, remap_weights, preferred_element_type=jnp.float32)

time: 184 us -> 188 us (1.022)
  waiting for transfers between devices: 64.8 us -> 91.8 us
  blocking collectives: 22.4 us -> 0 us
  starting transfers between devices: 28.5 us -> 32.5 us
  local copies, waits for them, and re-layouts: 39.6 us -> 36.3 us
    ppermute x0 -> x7, waiting for transfers between devices: none -> 24.3 us  [per_device(): parts = [lax.ppermute(parts[0], 'ox', forward_2), *parts]]
    all_gather x1 -> x0, blocking collectives: 22.4 us -> none  [per_device(): whole = lax.all_gather(atm_flux, 'ox', axis=2, tiled=True)]
    ppermute x0 -> x7, starting transfers between devices: none -> 7.22 us  [per_device(): parts = [lax.ppermute(parts[0], 'ox', forward_2), *parts]]
    ppermute x6, starting transfers between devices: 20.7 us -> 17.5 us  [with_halo(): lax.ppermute(lax.slice_in_dim(block, block.shape[dim] - width, None, axis...]
    reduce_scatter x1, waiting for transfers between devices: 55.7 us -> 58.8 us  [per_device(): lax.psum_scatter(dense, 'ox', scatter_dimension=1, tiled=True)]
  transfers between devices with their start and end apart: 13 -> 20, of which waited for: 5 -> 10; matrix products, arithmetic and copies ran while one was open for 8% -> 11% of each run, Pallas kernels for 0% -> 0%
where the time goes in v1:
time: 188 us; the launch traced here: 187 us
  waiting for transfers between devices  91.8 us (49%)
  local copies, waits for them, and re-layouts  36.3 us (19%)
  starting transfers between devices  32.5 us (17%)
  between operations  14.8 us (8%)
  other arithmetic  10.5 us (6%)
    reduce_scatter x1, waiting for transfers between devices, per_device(): lax.psum_scatter(dense, 'ox', scatter_dimension=1, tiled=True)  58.8 us
    ppermute x7, waiting for transfers between devices, per_device(): parts = [lax.ppermute(parts[0], 'ox', forward_2), *parts]  24.3 us
    ppermute x6, starting transfers between devices, with_halo(): lax.ppermute(lax.slice_in_dim(block, block.shape[dim] - width, None, axis...  17.5 us
    slice x9, local copies, waits for them, and re-layouts, with_halo(): lax.slice_in_dim(block, block.shape[dim] - width, None, axis=dim)  10.7 us
    ppermute x6, starting transfers between devices, with_halo(): lax.ppermute(lax.slice_in_dim(block, 0, width, axis=dim), axis, backward)  7.72 us
    ppermute x6, waiting for transfers between devices, with_halo(): lax.ppermute(lax.slice_in_dim(block, 0, width, axis=dim), axis, backward)  7.57 us
    ppermute x7, starting transfers between devices, per_device(): parts = [lax.ppermute(parts[0], 'ox', forward_2), *parts]  7.22 us
    another operation x3, other arithmetic, advance(): pressure = jnp.cumsum(density, axis=0) - 0.5 * density  6.62 us
  transfers between devices with their start and end apart: 20, of which 10 were waited for; matrix products, arithmetic and copies ran while one was open for 11% of the time, Pallas kernels for 0%

profile of v1, /device:TPU:0, one launch (start us, length us, event | category | flops | bytes accessed | tf_op | source)
XLA Modules:
  0.0 187.2 jit_solution(10653873714528077479)
XLA Ops:
  7.2 3.0 %collective-permute-start.4 = (bf16[4,10,128]{2,0,1:T(4,128)(2,1)}, bf16[4,10,128]{2,0,1:T(4,128)(2,1)S(1)}, u32[]{:S(2)}, u32[]{:S(2)}) collective-permute-start(bf16[4,10,128]{2,0,1:T(4,128)(2,1)} %param.14), channel_id=1, source_target_pairs={{0,4},{4,8},{8,12},{12,16},{16,20},{20,24},{24,28},{28,0},{1,5},{5... | collective-permute-start | bytes 30728 | tf_op jit(solution)/shard_map/ppermute | solution.py:88
  11.3 3.5 %collective-permute-start.1 = (f32[4,16,1,128]{3,2,1,0:T(1,128)S(1)}, f32[4,16,1,128]{3,2,1,0:T(1,128)S(1)}, u32[]{:S(2)}, u32[]{:S(2)}) collective-permute-start(f32[4,16,1,128]{3,2,1,0:T(1,128)S(1)} %get-tuple-element.76), channel_id=1, source_target_pairs={{0,4},{4,8},{8,12},{12,16},{16,20},{20,24},{24,28},{1,5},{5,9},{9,... | collective-permute-start | bytes 98312 | tf_op jit(solution)/shard_map/ppermute | solution.py:21
  14.8 1.3 collective-permute-start
  16.9 1.7 slice_bitcast_fusion.5
  18.6 2.3 %fusion.84 = (f32[4,15,16,128]{3,2,1,0:T(8,128)}, f32[4,15,16,128]{3,2,1,0:T(8,128)}) fusion(f32[4,16,16,128]{3,2,1,0:T(8,128)} %param.18), kind=kLoop, calls=%fused_computation.180 | loop fusion | bytes 1966080 | tf_op jit(solution)/shard_map/slice | solution.py:41
  22.2 2.7 %collective-permute-start.5 = (bf16[4,10,128]{2,0,1:T(4,128)(2,1)S(1)}, bf16[4,10,128]{2,0,1:T(4,128)(2,1)S(1)}, u32[]{:S(2)}, u32[]{:S(2)}) collective-permute-start(bf16[4,10,128]{2,0,1:T(4,128)(2,1)S(1)} %collective-permute-done.4), channel_id=1, source_target_pairs={{0,4},{4,8},{8,12},{12,16},{16,20},{20,24},{24,28},{28,0},{1,5},{5... | collective-permute-start | bytes 30728 | tf_op jit(solution)/shard_map/ppermute | solution.py:88
  25.0 3.6 %collective-permute-done.5 = bf16[4,10,128]{2,0,1:T(4,128)(2,1)S(1)} collective-permute-done((bf16[4,10,128]{2,0,1:T(4,128)(2,1)S(1)}, bf16[4,10,128]{2,0,1:T(4,128)(2,1)S(1)}, u32[]{:S(2)}, u32[]{:S(2)}) %collective-permute-start.5) | collective-permute-done | bytes 10272 | tf_op jit(solution)/shard_map/ppermute | solution.py:88
  28.7 6.3 %collective-permute-done.6 = bf16[4,10,128]{2,0,1:T(4,128)(2,1)S(1)} collective-permute-done((bf16[4,10,128]{2,0,1:T(4,128)(2,1)S(1)}, bf16[4,10,128]{2,0,1:T(4,128)(2,1)S(1)}, u32[]{:S(2)}, u32[]{:S(2)}) %collective-permute-start.6) | collective-permute-done | bytes 10272 | tf_op jit(solution)/shard_map/ppermute | solution.py:88
  36.4 1.6 copy.144
  38.5 1.3 collective-permute-start.2
  39.8 3.0 %collective-permute-start.3 = (f32[4,16,18,1]{2,1,3,0:T(8,128)S(1)}, f32[4,16,18,1]{2,1,3,0:T(8,128)S(1)}, u32[]{:S(2)}, u32[]{:S(2)}) collective-permute-start(f32[4,16,18,1]{2,1,3,0:T(8,128)S(1)} %copy.144), channel_id=1, source_target_pairs={{0,1},{1,2},{2,3},{4,5},{5,6},{6,7},{8,9},{9,10},{10,11},{12,13},{... | collective-permute-start | bytes 13832 | tf_op jit(solution)/shard_map/ppermute | solution.py:21
  44.7 1.4 copy.143
  46.1 1.5 collective-permute-start.8
  47.6 2.2 %reduce-window_subtract_fusion.2 = f32[16,18,130]{2,1,0:T(8,128)S(1)} fusion(f32[4,16,18,1]{3,2,1,0:T(8,128)} %copy.143, f32[4,16,1,128]{3,2,1,0:T(1,128)S(1)} %collective-permute-done, f32[4,16,16,128]{3,2,1,0:T(8,128)S(1)} %copy-done.2, f32[4,16,1,128]{3,2,1,0:T(1,128)S(1)} %collective-permute-done.1, f32[4,16,18,1]{3,2,1,0:T(8,128)S(1)} %copy.145), kind=kOutput, calls=%fused_computation.4 | output fusion | flops 1460160 | bytes 748800 | tf_op jit(solution)/shard_map/jit(cumsum)/reduce_window_sum | solution.py:44
  49.8 2.8 %collective-permute-done.8 = bf16[4,10,128]{2,0,1:T(4,128)(2,1)S(1)} collective-permute-done((bf16[4,10,128]{2,0,1:T(4,128)(2,1)S(1)}, bf16[4,10,128]{2,0,1:T(4,128)(2,1)S(1)}, u32[]{:S(2)}, u32[]{:S(2)}) %collective-permute-start.8) | collective-permute-done | bytes 10272 | tf_op jit(solution)/shard_map/ppermute | solution.py:88
  52.7 6.2 %collective-permute-done.9 = bf16[4,10,128]{2,0,1:T(4,128)(2,1)S(1)} collective-permute-done((bf16[4,10,128]{2,0,1:T(4,128)(2,1)S(1)}, bf16[4,10,128]{2,0,1:T(4,128)(2,1)S(1)}, u32[]{:S(2)}, u32[]{:S(2)}) %collective-permute-start.9) | collective-permute-done | bytes 10272 | tf_op jit(solution)/shard_map/ppermute | solution.py:88
  59.9 5.4 %collective-permute-done.10 = bf16[4,10,128]{2,0,1:T(4,128)(2,1)S(1)} collective-permute-done((bf16[4,10,128]{2,0,1:T(4,128)(2,1)S(1)}, bf16[4,10,128]{2,0,1:T(4,128)(2,1)S(1)}, u32[]{:S(2)}, u32[]{:S(2)}) %collective-permute-start.10) | collective-permute-done | bytes 10272 | tf_op jit(solution)/shard_map/ppermute | solution.py:88
  69.2 1.3 collective-permute-start.11
  71.3 3.8 %collective-permute-done.11 = f32[4,16,1,128]{3,2,1,0:T(1,128)S(1)} collective-permute-done((f32[4,16,1,128]{3,2,1,0:T(1,128)S(1)}, f32[4,16,1,128]{3,2,1,0:T(1,128)S(1)}, u32[]{:S(2)}, u32[]{:S(2)}) %collective-permute-start.11) | collective-permute-done | bytes 32800 | tf_op jit(solution)/shard_map/ppermute | solution.py:24
  76.4 2.2 %copy.156 = f32[4,16,18,1]{2,1,3,0:T(8,128)} copy(f32[4,16,18,1]{3,2,1,0:T(8,128)} %get-tuple-element.54) | data formatting | bytes 9216 | tf_op jit(solution)/shard_map/slice | solution.py:22
  79.6 1.3 collective-permute-start.13
  80.9 3.6 %collective-permute-start.14 = (f32[4,16,18,1]{2,1,3,0:T(8,128)}, f32[4,16,18,1]{2,1,3,0:T(8,128)}, u32[]{:S(2)}, u32[]{:S(2)}) collective-permute-start(f32[4,16,18,1]{2,1,3,0:T(8,128)} %copy.156), channel_id=1, source_target_pairs={{0,1},{1,2},{2,3},{4,5},{5,6},{6,7},{8,9},{9,10},{10,11},{12,13},{... | collective-permute-start | bytes 13832 | tf_op jit(solution)/shard_map/ppermute | solution.py:21
  86.4 2.1 %copy.155 = f32[4,16,18,1]{3,2,1,0:T(8,128)} copy(f32[4,16,18,1]{2,1,3,0:T(8,128)} %collective-permute-done.13) | data formatting | bytes 9216 | tf_op jit(solution)/shard_map/ppermute | solution.py:24
  88.6 2.2 %reduce-window_subtract_fusion.1 = f32[16,18,130]{2,1,0:T(8,128)S(1)} fusion(f32[4,16,18,1]{3,2,1,0:T(8,128)} %copy.155, f32[4,16,1,128]{3,2,1,0:T(1,128)S(1)} %collective-permute-done.11, f32[4,16,16,128]{3,2,1,0:T(8,128)S(1)} %multiply_add_fusion.2, f32[4,16,1,128]{3,2,1,0:T(1,128)S(1)} %collective-permute-done.12, f32[4,16,18,1]{3,2,1,0:T(8,128)S(1)} %copy.157), kind=kOutput, calls=%fused_computation.3 | output fusion | flops 1460160 | bytes 748800 | tf_op jit(solution)/shard_map/jit(cumsum)/reduce_window_sum | solution.py:44
  93.9 1.6 collective-permute-start.16
  95.5 1.3 collective-permute-start.15
  97.5 3.8 %collective-permute-done.15 = f32[4,16,1,128]{3,2,1,0:T(1,128)S(1)} collective-permute-done((f32[4,16,1,128]{3,2,1,0:T(1,128)S(1)}, f32[4,16,1,128]{3,2,1,0:T(1,128)S(1)}, u32[]{:S(2)}, u32[]{:S(2)}) %collective-permute-start.15) | collective-permute-done | bytes 32800 | tf_op jit(solution)/shard_map/ppermute | solution.py:24
  102.6 2.2 %copy.162 = f32[4,16,18,1]{2,1,3,0:T(8,128)} copy(f32[4,16,18,1]{3,2,1,0:T(8,128)} %get-tuple-element.52) | data formatting | bytes 9216 | tf_op jit(solution)/shard_map/slice | solution.py:22
  107.2 4.5 %collective-permute-start.18 = (f32[4,16,18,1]{2,1,3,0:T(8,128)}, f32[4,16,18,1]{2,1,3,0:T(8,128)}, u32[]{:S(2)}, u32[]{:S(2)}) collective-permute-start(f32[4,16,18,1]{2,1,3,0:T(8,128)} %copy.162), channel_id=1, source_target_pairs={{0,1},{1,2},{2,3},{4,5},{5,6},{6,7},{8,9},{9,10},{10,11},{12,13},{... | collective-permute-start | bytes 13832 | tf_op jit(solution)/shard_map/ppermute | solution.py:21
  113.5 2.1 %copy.161 = f32[4,16,18,1]{3,2,1,0:T(8,128)} copy(f32[4,16,18,1]{2,1,3,0:T(8,128)} %collective-permute-done.17) | data formatting | bytes 9216 | tf_op jit(solution)/shard_map/ppermute | solution.py:24
  115.7 2.2 %reduce-window_subtract_fusion = f32[16,18,130]{2,1,0:T(8,128)S(1)} fusion(f32[4,16,18,1]{3,2,1,0:T(8,128)} %copy.161, f32[4,16,1,128]{3,2,1,0:T(1,128)S(1)} %collective-permute-done.15, f32[4,16,16,128]{3,2,1,0:T(8,128)S(1)} %multiply_add_fusion.1, f32[4,16,1,128]{3,2,1,0:T(1,128)S(1)} %collective-permute-done.16, f32[4,16,18,1]{3,2,1,0:T(8,128)S(1)} %copy.163), kind=kOutput, calls=%fused_computation.2 | output fusion | flops 1460160 | bytes 748800 | tf_op jit(solution)/shard_map/jit(cumsum)/reduce_window_sum | solution.py:44
  121.6 58.8 %reduce-scatter.2.cloned.1.call-done = f32[10,128]{1,0:T(8,128)} async-done(((f32[10,1024]{1,0:T(8,128)}), f32[10,128]{1,0:T(8,128)}) %reduce-scatter.2.cloned.1.call-update) | async-done | bytes 5136 | tf_op jit(solution)/shard_map/reduce_scatter | solution.py:114
  (167 shorter events, 29.7 us)
Async XLA Ops:
  7.2 59.1 %copy-start = (bf16[16,3,128,128]{3,2,1,0:T(8,128)(2,1)S(1)}, bf16[16,3,128,128]{3,2,1,0:T(8,128)(2,1)}, u32[]{:S(2)}) copy-start(bf16[16,3,128,128]{3,2,1,0:T(8,128)(2,1)} %param.15) | copy-start | bytes 4718596
  7.2 13.7 %copy-start.36 = (s32[16,3]{0,1:T(4,128)S(1)}, s32[16,3]{0,1:T(4,128)}, u32[]{:S(2)}) copy-start(s32[16,3]{0,1:T(4,128)} %param.16) | copy-start | bytes 580
  7.2 13.9 %copy-start.1 = (s32[8,3]{0,1:T(4,128)S(1)}, s32[8,3]{0,1:T(4,128)}, u32[]{:S(2)}) copy-start(s32[8,3]{0,1:T(4,128)} %param.17) | copy-start | bytes 292
  7.2 173.1 %reduce-scatter.2.cloned.1.call-start = ((), (), s32[]{:S(2)}) async-start(), calls=%async_computation.1 | async-start | bytes 73728 | tf_op jit(solution)/shard_map/reduce_scatter | solution.py:114
  7.2 15.0 %collective-permute-start.4 = (bf16[4,10,128]{2,0,1:T(4,128)(2,1)}, bf16[4,10,128]{2,0,1:T(4,128)(2,1)S(1)}, u32[]{:S(2)}, u32[]{:S(2)}) collective-permute-start(bf16[4,10,128]{2,0,1:T(4,128)(2,1)} %param.14), channel_id=1, source_target_pairs={{0,4},{4,8},{8,12},{12,16},{16,20},{20,24},{24,28},{28,0},{1,5},{5... | collective-permute-start | bytes 30728 | tf_op jit(solution)/shard_map/ppermute | solution.py:88
  11.3 23.7 %collective-permute-start.1 = (f32[4,16,1,128]{3,2,1,0:T(1,128)S(1)}, f32[4,16,1,128]{3,2,1,0:T(1,128)S(1)}, u32[]{:S(2)}, u32[]{:S(2)}) collective-permute-start(f32[4,16,1,128]{3,2,1,0:T(1,128)S(1)} %get-tuple-element.76), channel_id=1, source_target_pairs={{0,4},{4,8},{8,12},{12,16},{16,20},{20,24},{24,28},{1,5},{5,9},{9,... | collective-permute-start | bytes 98312 | tf_op jit(solution)/shard_map/ppermute | solution.py:21
  14.8 20.3 %collective-permute-start = (f32[4,16,1,128]{3,2,1,0:T(1,128)S(1)}, f32[4,16,1,128]{3,2,1,0:T(1,128)S(1)}, u32[]{:S(2)}, u32[]{:S(2)}) collective-permute-start(f32[4,16,1,128]{3,2,1,0:T(1,128)S(1)} %get-tuple-element.77), channel_id=1, source_target_pairs={{4,0},{8,4},{12,8},{16,12},{20,16},{24,20},{28,24},{5,1},{9,5},{13... | collective-permute-start | bytes 98312 | tf_op jit(solution)/shard_map/ppermute | solution.py:24
  21.0 14.0 %copy-start.2 = (f32[4,16,16,128]{3,2,1,0:T(8,128)S(1)}, f32[4,16,16,128]{3,2,1,0:T(8,128)}, u32[]{:S(2)}) copy-start(f32[4,16,16,128]{3,2,1,0:T(8,128)} %param.18) | copy-start | bytes 1572868
  22.2 12.8 %copy-start.18 = (bf16[4,10,128]{2,0,1:T(4,128)(2,1)}, bf16[4,10,128]{2,0,1:T(4,128)(2,1)S(1)}, u32[]{:S(2)}) copy-start(bf16[4,10,128]{2,0,1:T(4,128)(2,1)S(1)} %collective-permute-done.4) | copy-start | bytes 30724
  22.2 6.4 %collective-permute-start.5 = (bf16[4,10,128]{2,0,1:T(4,128)(2,1)S(1)}, bf16[4,10,128]{2,0,1:T(4,128)(2,1)S(1)}, u32[]{:S(2)}, u32[]{:S(2)}) collective-permute-start(bf16[4,10,128]{2,0,1:T(4,128)(2,1)S(1)} %collective-permute-done.4), channel_id=1, source_target_pairs={{0,4},{4,8},{8,12},{12,16},{16,20},{20,24},{24,28},{28,0},{1,5},{5... | collective-permute-start | bytes 30728 | tf_op jit(solution)/shard_map/ppermute | solution.py:88
  28.7 6.4 %collective-permute-start.6 = (bf16[4,10,128]{2,0,1:T(4,128)(2,1)S(1)}, bf16[4,10,128]{2,0,1:T(4,128)(2,1)S(1)}, u32[]{:S(2)}, u32[]{:S(2)}) collective-permute-start(bf16[4,10,128]{2,0,1:T(4,128)(2,1)S(1)} %collective-permute-done.5), channel_id=1, source_target_pairs={{0,4},{4,8},{8,12},{12,16},{16,20},{20,24},{24,28},{28,0},{1,5},{5... | collective-permute-start | bytes 30728 | tf_op jit(solution)/shard_map/ppermute | solution.py:88
  35.0 11.1 %collective-permute-start.7 = (bf16[4,10,128]{2,0,1:T(4,128)(2,1)S(1)}, bf16[4,10,128]{2,0,1:T(4,128)(2,1)S(1)}, u32[]{:S(2)}, u32[]{:S(2)}) collective-permute-start(bf16[4,10,128]{2,0,1:T(4,128)(2,1)S(1)} %collective-permute-done.6), channel_id=1, source_target_pairs={{0,4},{4,8},{8,12},{12,16},{16,20},{20,24},{24,28},{28,0},{1,5},{5... | collective-permute-start | bytes 30728 | tf_op jit(solution)/shard_map/ppermute | solution.py:88
  38.5 6.2 %collective-permute-start.2 = (f32[4,16,18,1]{2,1,3,0:T(8,128)S(1)}, f32[4,16,18,1]{2,1,3,0:T(8,128)S(1)}, u32[]{:S(2)}, u32[]{:S(2)}) collective-permute-start(f32[4,16,18,1]{2,1,3,0:T(8,128)S(1)} %copy.142), channel_id=1, source_target_pairs={{1,0},{2,1},{3,2},{5,4},{6,5},{7,6},{9,8},{10,9},{11,10},{13,12},{... | collective-permute-start | bytes 13832 | tf_op jit(solution)/shard_map/ppermute | solution.py:24
  39.8 4.4 %collective-permute-start.3 = (f32[4,16,18,1]{2,1,3,0:T(8,128)S(1)}, f32[4,16,18,1]{2,1,3,0:T(8,128)S(1)}, u32[]{:S(2)}, u32[]{:S(2)}) collective-permute-start(f32[4,16,18,1]{2,1,3,0:T(8,128)S(1)} %copy.144), channel_id=1, source_target_pairs={{0,1},{1,2},{2,3},{4,5},{5,6},{6,7},{8,9},{9,10},{10,11},{12,13},{... | collective-permute-start | bytes 13832 | tf_op jit(solution)/shard_map/ppermute | solution.py:21
  46.1 12.9 %copy-start.6 = (f32[4,15,16,128]{3,2,1,0:T(8,128)S(1)}, f32[4,15,16,128]{3,2,1,0:T(8,128)}, u32[]{:S(2)}) copy-start(f32[4,15,16,128]{3,2,1,0:T(8,128)} %get-tuple-element.78) | copy-start | bytes 1474564
  46.1 12.9 %copy-start.7 = (f32[4,15,16,128]{3,2,1,0:T(8,128)S(1)}, f32[4,15,16,128]{3,2,1,0:T(8,128)}, u32[]{:S(2)}) copy-start(f32[4,15,16,128]{3,2,1,0:T(8,128)} %get-tuple-element.79) | copy-start | bytes 1474564
  46.1 12.9 %copy-start.11 = (f32[16,16,128]{2,1,0:T(8,128)S(1)}, f32[16,16,128]{2,1,0:T(8,128)}, u32[]{:S(2)}) copy-start(f32[16,16,128]{2,1,0:T(8,128)} %get-tuple-element.74) | copy-start | bytes 393220
  46.1 12.9 %copy-start.12 = (f32[16,16,128]{2,1,0:T(8,128)S(1)}, f32[16,16,128]{2,1,0:T(8,128)}, u32[]{:S(2)}) copy-start(f32[16,16,128]{2,1,0:T(8,128)} %get-tuple-element.75) | copy-start | bytes 393220
  46.1 12.9 %copy-start.29 = (f32[16]{0:T(128)S(1)}, f32[16]{0:T(128)}, u32[]{:S(2)}) copy-start(f32[16]{0:T(128)} %param.20) | copy-start | bytes 196
  46.1 12.9 %copy-start.32 = (f32[4]{0:T(128)S(1)}, f32[4]{0:T(128)}, u32[]{:S(2)}) copy-start(f32[4]{0:T(128)} %pad.62.clone) | copy-start | bytes 52
  46.1 6.4 %collective-permute-start.8 = (bf16[4,10,128]{2,0,1:T(4,128)(2,1)S(1)}, bf16[4,10,128]{2,0,1:T(4,128)(2,1)S(1)}, u32[]{:S(2)}, u32[]{:S(2)}) collective-permute-start(bf16[4,10,128]{2,0,1:T(4,128)(2,1)S(1)} %collective-permute-done.7), channel_id=1, source_target_pairs={{0,4},{4,8},{8,12},{12,16},{16,20},{20,24},{24,28},{28,0},{1,5},{5... | collective-permute-start | bytes 30728 | tf_op jit(solution)/shard_map/ppermute | solution.py:88
  52.5 6.4 %collective-permute-start.9 = (bf16[4,10,128]{2,0,1:T(4,128)(2,1)S(1)}, bf16[4,10,128]{2,0,1:T(4,128)(2,1)S(1)}, u32[]{:S(2)}, u32[]{:S(2)}) collective-permute-start(bf16[4,10,128]{2,0,1:T(4,128)(2,1)S(1)} %collective-permute-done.8), channel_id=1, source_target_pairs={{0,4},{4,8},{8,12},{12,16},{16,20},{20,24},{24,28},{28,0},{1,5},{5... | collective-permute-start | bytes 30728 | tf_op jit(solution)/shard_map/ppermute | solution.py:88
  58.9 6.4 %collective-permute-start.10 = (bf16[4,10,128]{2,0,1:T(4,128)(2,1)S(1)}, bf16[4,10,128]{2,0,1:T(4,128)(2,1)S(1)}, u32[]{:S(2)}, u32[]{:S(2)}) collective-permute-start(bf16[4,10,128]{2,0,1:T(4,128)(2,1)S(1)} %collective-permute-done.9), channel_id=1, source_target_pairs={{0,4},{4,8},{8,12},{12,16},{16,20},{20,24},{24,28},{28,0},{1,5},{5... | collective-permute-start | bytes 30728 | tf_op jit(solution)/shard_map/ppermute | solution.py:88
  68.0 3.3 %collective-permute-start.12 = (f32[4,16,1,128]{3,2,1,0:T(1,128)S(1)}, f32[4,16,1,128]{3,2,1,0:T(1,128)S(1)}, u32[]{:S(2)}, u32[]{:S(2)}) collective-permute-start(f32[4,16,1,128]{3,2,1,0:T(1,128)S(1)} %get-tuple-element.68), channel_id=1, source_target_pairs={{0,4},{4,8},{8,12},{12,16},{16,20},{20,24},{24,28},{1,5},{5,9},{9,... | collective-permute-start | bytes 98312 | tf_op jit(solution)/shard_map/ppermute | solution.py:21
  69.2 5.8 %collective-permute-start.11 = (f32[4,16,1,128]{3,2,1,0:T(1,128)S(1)}, f32[4,16,1,128]{3,2,1,0:T(1,128)S(1)}, u32[]{:S(2)}, u32[]{:S(2)}) collective-permute-start(f32[4,16,1,128]{3,2,1,0:T(1,128)S(1)} %get-tuple-element.69), channel_id=1, source_target_pairs={{4,0},{8,4},{12,8},{16,12},{20,16},{24,20},{28,24},{5,1},{9,5},{13... | collective-permute-start | bytes 98312 | tf_op jit(solution)/shard_map/ppermute | solution.py:24
  79.6 6.8 %collective-permute-start.13 = (f32[4,16,18,1]{2,1,3,0:T(8,128)}, f32[4,16,18,1]{2,1,3,0:T(8,128)}, u32[]{:S(2)}, u32[]{:S(2)}) collective-permute-start(f32[4,16,18,1]{2,1,3,0:T(8,128)} %copy.154), channel_id=1, source_target_pairs={{1,0},{2,1},{3,2},{5,4},{6,5},{7,6},{9,8},{10,9},{11,10},{13,12},{... | collective-permute-start | bytes 13832 | tf_op jit(solution)/shard_map/ppermute | solution.py:24
  80.9 4.2 %collective-permute-start.14 = (f32[4,16,18,1]{2,1,3,0:T(8,128)}, f32[4,16,18,1]{2,1,3,0:T(8,128)}, u32[]{:S(2)}, u32[]{:S(2)}) collective-permute-start(f32[4,16,18,1]{2,1,3,0:T(8,128)} %copy.156), channel_id=1, source_target_pairs={{0,1},{1,2},{2,3},{4,5},{5,6},{6,7},{8,9},{9,10},{10,11},{12,13},{... | collective-permute-start | bytes 13832 | tf_op jit(solution)/shard_map/ppermute | solution.py:21
  93.9 3.6 %collective-permute-start.16 = (f32[4,16,1,128]{3,2,1,0:T(1,128)S(1)}, f32[4,16,1,128]{3,2,1,0:T(1,128)S(1)}, u32[]{:S(2)}, u32[]{:S(2)}) collective-permute-start(f32[4,16,1,128]{3,2,1,0:T(1,128)S(1)} %get-tuple-element.60), channel_id=1, source_target_pairs={{0,4},{4,8},{8,12},{12,16},{16,20},{20,24},{24,28},{1,5},{5,9},{9,... | collective-permute-start | bytes 98312 | tf_op jit(solution)/shard_map/ppermute | solution.py:21
  95.5 5.8 %collective-permute-start.15 = (f32[4,16,1,128]{3,2,1,0:T(1,128)S(1)}, f32[4,16,1,128]{3,2,1,0:T(1,128)S(1)}, u32[]{:S(2)}, u32[]{:S(2)}) collective-permute-start(f32[4,16,1,128]{3,2,1,0:T(1,128)S(1)} %get-tuple-element.61), channel_id=1, source_target_pairs={{4,0},{8,4},{12,8},{16,12},{20,16},{24,20},{28,24},{5,1},{9,5},{13... | collective-permute-start | bytes 98312 | tf_op jit(solution)/shard_map/ppermute | solution.py:24
  105.9 7.6 %collective-permute-start.17 = (f32[4,16,18,1]{2,1,3,0:T(8,128)}, f32[4,16,18,1]{2,1,3,0:T(8,128)}, u32[]{:S(2)}, u32[]{:S(2)}) collective-permute-start(f32[4,16,18,1]{2,1,3,0:T(8,128)} %copy.160), channel_id=1, source_target_pairs={{1,0},{2,1},{3,2},{5,4},{6,5},{7,6},{9,8},{10,9},{11,10},{13,12},{... | collective-permute-start | bytes 13832 | tf_op jit(solution)/shard_map/ppermute | solution.py:24
  107.2 5.1 %collective-permute-start.18 = (f32[4,16,18,1]{2,1,3,0:T(8,128)}, f32[4,16,18,1]{2,1,3,0:T(8,128)}, u32[]{:S(2)}, u32[]{:S(2)}) collective-permute-start(f32[4,16,18,1]{2,1,3,0:T(8,128)} %copy.162), channel_id=1, source_target_pairs={{0,1},{1,2},{2,3},{4,5},{5,6},{6,7},{8,9},{9,10},{10,11},{12,13},{... | collective-permute-start | bytes 13832 | tf_op jit(solution)/shard_map/ppermute | solution.py:21
  120.0 60.3 %copy-start.10 = (f32[4,16,16,128]{3,2,1,0:T(8,128)}, f32[4,16,16,128]{3,2,1,0:T(8,128)S(1)}, u32[]{:S(2)}) copy-start(f32[4,16,16,128]{3,2,1,0:T(8,128)S(1)} %multiply_add_fusion) | copy-start | bytes 1572868
  (25 other events, 98.6 us)
Sparse Core Ops, SparseCore 0:
  121.7 58.5 reduce-scatter.1
